TPU v7x, 32 devices: a whole 2x2x4 slice. The times are simulated.
32 devices in a mesh: tm: 16 (over z, y, x), sec: 2 (over core).
Axes of the slice: x: 2, y: 2, z: 4, core: 2. Of those that a mesh axis runs over, the one named last changes fastest.
Arguments:
- signal: bfloat16 [2048, 16384], P('sec', 'tm')
- round_shard: int32 [2], replicated, may hold values from 0 to 15
- offsets: int32 [2, 16], replicated, may hold values from 0 to 896
- chan_range: int32 [2, 16, 2], replicated, may hold values from 0 to 2048, as said below
Outputs:
- detection: float32 [2, 16, 16384], P(None, None, 'tm')
Inputs may be any that keep to these rules, and one draw needn't show every extreme that they name: chan_range[r, k] = (lo, hi) with lo < hi and hi - lo >= 512.
All inputs are finite; a program needn't handle non-finite values.
Results may differ from a plain program's by a relative error of at most 0.0003.
Values may be sent and summed in bfloat16 or wider, within the bound.
No kernel may reach another device: no remote copies, remote signals or barrier semaphores. Data moves between devices by JAX's collectives and lax.ppermute only.
A program may use at most 64 MiB of HBM per device.

v0:
```python
import jax
import jax.numpy as jnp
from jax import lax
from jax.sharding import PartitionSpec as P

L = 128
TPL_BLOCK = 4
ROUNDS = 2
EPS = 1e-06


def from_behind(value, axis, by):
    length = lax.axis_size(axis)
    pairs = [(i, i + by) for i in range(length) if 0 <= i + by < length]
    return lax.ppermute(value, axis, pairs)


def spread(value, axis, source):
    kept = jnp.where(lax.axis_index(axis) == source, value, 0).astype(value.dtype)
    return lax.psum(kept, axis)


def skew_sum(product, lag_count):
    group_count, tap_count, span_width = product.shape
    flipped = product[:, :, ::-1]
    widened = jnp.pad(flipped, ((0, 0), (0, 0), (0, 1)))
    sheared = widened.reshape(group_count, tap_count * (span_width + 1))[
        :, : tap_count * span_width
    ]
    sheared = sheared.reshape(group_count, tap_count, span_width)
    summed = jnp.sum(sheared, axis=1)
    return summed[:, span_width - lag_count :][:, ::-1]


def correlate(templates, extended, lag_count):
    template_count = templates.shape[0]
    grouped = templates.reshape(
        template_count // TPL_BLOCK, TPL_BLOCK, templates.shape[1], templates.shape[2]
    )

    def one_block(block):
        product = jnp.einsum("kcl,cw->klw", block, extended, preferred_element_type=jnp.float32)
        return skew_sum(product, lag_count)

    return lax.map(one_block, grouped).reshape(template_count, lag_count)


def sliding_energy(masks, extended, lag_count, tap_count):
    squares = jnp.square(extended.astype(jnp.float32))
    summed = jnp.dot(
        masks, squares, precision=lax.Precision.HIGHEST, preferred_element_type=jnp.float32
    )
    running = jnp.pad(jnp.cumsum(summed, axis=1), ((0, 0), (1, 0)))
    return running[:, tap_count : tap_count + lag_count] - running[:, :lag_count]


def cut_windows(records, starts, inside):
    windows = jax.vmap(lambda first: lax.dynamic_slice_in_dim(records, first, L, axis=1))(starts)
    return jnp.where(inside[:, :, None], windows, jnp.zeros_like(windows))


def shards(signal, round_shard, offsets, chan_range):
    chan_local = signal.shape[0]
    lag_count = signal.shape[1]
    section = lax.axis_index("sec")
    total_lags = lag_count * lax.axis_size("tm")
    right_rim = from_behind(signal[:, :L], "tm", -1)
    extended = jnp.concatenate([signal, right_rim], axis=1)
    channel = section * chan_local + jnp.arange(chan_local, dtype=jnp.int32)

    def make_template(level):
        lower = chan_range[level, :, 0]
        upper = chan_range[level, :, 1]
        inside = (channel[None, :] >= lower[:, None]) & (channel[None, :] < upper[:, None])
        local_tmpl = cut_windows(signal, offsets[level], inside)
        templates = spread(local_tmpl, "tm", round_shard[level])
        local_power = jnp.sum(jnp.square(templates.astype(jnp.float32)), axis=(1, 2))
        tmpl_power = lax.psum(local_power, "sec")
        return (templates, inside.astype(jnp.float32), tmpl_power)

    def finish(templates, masks, tmpl_power):
        corr_local = correlate(templates, extended, lag_count)
        energy_local = sliding_energy(masks, extended, lag_count, L)
        corr, energy = lax.psum((corr_local, energy_local), "sec")
        normed = corr / jnp.sqrt(energy * tmpl_power[:, None] + EPS)
        power_sum = lax.psum(jnp.sum(normed * normed, axis=1), "tm")
        meansq = power_sum / total_lags
        scored = normed / jnp.sqrt(meansq[:, None] + EPS)
        return scored

    results = [finish(*make_template(level)) for level in range(ROUNDS)]
    return jnp.stack(results, axis=0)


def solution(mesh):
    placed = (P("sec", "tm"), P(), P(), P())
    return jax.shard_map(
        shards, mesh=mesh, in_specs=placed, out_specs=P(None, None, "tm"), check_vma=False
    )
```

profile of v0, /device:TPU:0, one launch (start us, length us, event | category | flops | bytes accessed | tf_op | source)
XLA Modules:
  0.0 749.8 jit_solution(7222854212829165390)
XLA Ops:
  13.5 49.9 %while.28 = (s32[]{:T(128)}, bf16[1024,1024]{1,0:T(8,128)(2,1)}, s32[16,2]{0,1:T(2,128)S(1)}, bf16[16,1024,128]{2,1,0:T(8,128)(2,1)}, s32[]{:T(128)}) while((s32[]{:T(128)}, bf16[1024,1024]{1,0:T(8,128)(2,1)}, s32[16,2]{0,1:T(2,128)S(1)}, bf16[16,1024,128]{2,1,0:T(8,128)(2,1)}, s32[]{:T(128)}) %tuple.84), condition=%wide.while_cond, body=%wide.while_body.sunk | while | flops 2 | bytes 525401 | solution.py:58
  66.2 49.9 %while.29 = (s32[]{:T(128)}, bf16[1024,1024]{1,0:T(8,128)(2,1)}, s32[16,2]{0,1:T(2,128)S(1)}, bf16[16,1024,128]{2,1,0:T(8,128)(2,1)}, s32[]{:T(128)}) while((s32[]{:T(128)}, bf16[1024,1024]{1,0:T(8,128)(2,1)}, s32[16,2]{0,1:T(2,128)S(1)}, bf16[16,1024,128]{2,1,0:T(8,128)(2,1)}, s32[]{:T(128)}) %tuple.102), condition=%wide.while_cond.1, body=%wide.while_body.1.sunk | while | flops 2 | bytes 525401 | solution.py:58
  116.2 8.0 %select_select_fusion = (bf16[16,1024,128]{2,1,0:T(8,128)(2,1)}, bf16[16,1024,128]{2,1,0:T(8,128)(2,1)}) fusion(bf16[16,1024,128]{2,1,0:T(8,128)(2,1)} %get-tuple-element.128, pred[16,1024]{1,0:T(8,128)(4,1)S(1)} %get-tuple-element.188, pred[]{:T(512)S(6)} %eq.7, bf16[16,1024,128]{2,1,0:T(8,128)(2,1)} %get-tuple-element.120, ...), kind=kLoop, calls=%fused_computation.23 | loop fusion | flops 8388608 | bytes 16809986 | tf_op jit(solution)/shard_map/jit(_where)/select_n | solution.py:19
  128.3 10.6 %collective-permute-done = bf16[1024,128]{1,0:T(8,128)(2,1)S(1)} collective-permute-done((bf16[1024,128]{1,0:T(8,128)(2,1)S(1)}, bf16[1024,128]{1,0:T(8,128)(2,1)S(1)}, u32[]{:S(2)}, u32[]{:S(2)}) %collective-permute-start) | collective-permute-done | bytes 262176 | tf_op jit(solution)/shard_map/ppermute | solution.py:15
  153.9 233.3 %all-reduce.15.cloned.1.call-done = (bf16[16,1024,128]{2,1,0:T(8,128)(2,1)}, bf16[16,1024,128]{2,1,0:T(8,128)(2,1)}) async-done(((bf16[16,1024,128]{2,1,0:T(8,128)(2,1)}, bf16[16,1024,128]{2,1,0:T(8,128)(2,1)}), (bf16[16,1024,128]{2,1,0:T(8,128)(2,1)}, bf16[16,1024,128]{2,1,0:T(8,128)(2,1)})) %all-reduce.15.cloned.1.call-update) | async-done | bytes 8388624 | tf_op jit(solution)/shard_map/psum | solution.py:20
  390.4 143.4 %while.26 = (s32[]{:T(128)}, f32[4,4,1024]{2,1,0:T(4,128)S(1)}, bf16[4,4,1024,128]{3,2,1,0:T(8,128)(2,1)}, bf16[1024,1152]{1,0:T(8,128)(2,1)S(1)}, s32[]{:T(128)}, /*index=5*/f32[]{:T(128)}) while((s32[]{:T(128)}, f32[4,4,1024]{2,1,0:T(4,128)S(1)}, bf16[4,4,1024,128]{3,2,1,0:T(8,128)(2,1)}, bf16[1024,1152]{1,0:T(8,128)(2,1)S(1)}, s32[]{:T(128)}, ...), condition=%wide.region_3.4_spmd, body=%wide.region_1.3_spmd.sunk | while | flops 1208544768 | bytes 29483620 | solution.py:45
  394.7 19.8 %rev.28 = f32[4,128,1152]{2,1,0:T(8,128)} reverse(f32[4,128,1152]{2,1,0:T(8,128)} %fusion.23), dimensions={2} | reverse | bytes 4718592 | tf_op jit(solution)/shard_map/while/body/eval_jaxpr/rev | solution.py:25
  418.0 5.8 reshape.302
  430.6 19.8 %rev.28 = f32[4,128,1152]{2,1,0:T(8,128)} reverse(f32[4,128,1152]{2,1,0:T(8,128)} %fusion.23), dimensions={2} | reverse | bytes 4718592 | tf_op jit(solution)/shard_map/while/body/eval_jaxpr/rev | solution.py:25
  453.8 5.8 reshape.302
  466.4 19.8 %rev.28 = f32[4,128,1152]{2,1,0:T(8,128)} reverse(f32[4,128,1152]{2,1,0:T(8,128)} %fusion.23), dimensions={2} | reverse | bytes 4718592 | tf_op jit(solution)/shard_map/while/body/eval_jaxpr/rev | solution.py:25
  489.6 5.8 reshape.302
  502.3 19.8 %rev.28 = f32[4,128,1152]{2,1,0:T(8,128)} reverse(f32[4,128,1152]{2,1,0:T(8,128)} %fusion.23), dimensions={2} | reverse | bytes 4718592 | tf_op jit(solution)/shard_map/while/body/eval_jaxpr/rev | solution.py:25
  525.5 5.8 reshape.302
  534.5 143.4 %while.27 = (s32[]{:T(128)}, f32[4,4,1024]{2,1,0:T(4,128)S(1)}, bf16[4,4,1024,128]{3,2,1,0:T(8,128)(2,1)}, bf16[1024,1152]{1,0:T(8,128)(2,1)S(1)}, s32[]{:T(128)}, /*index=5*/f32[]{:T(128)}) while((s32[]{:T(128)}, f32[4,4,1024]{2,1,0:T(4,128)S(1)}, bf16[4,4,1024,128]{3,2,1,0:T(8,128)(2,1)}, bf16[1024,1152]{1,0:T(8,128)(2,1)S(1)}, ...), condition=%wide.region_15.16_spmd, body=%wide.region_13.15_spmd.sunk | while | flops 1208544768 | bytes 29483620 | solution.py:45
  538.8 19.8 %rev.30 = f32[4,128,1152]{2,1,0:T(8,128)} reverse(f32[4,128,1152]{2,1,0:T(8,128)} %fusion.26), dimensions={2} | reverse | bytes 4718592 | tf_op jit(solution)/shard_map/while/body/eval_jaxpr/rev | solution.py:25
  562.0 5.8 reshape.303
  574.6 19.8 %rev.30 = f32[4,128,1152]{2,1,0:T(8,128)} reverse(f32[4,128,1152]{2,1,0:T(8,128)} %fusion.26), dimensions={2} | reverse | bytes 4718592 | tf_op jit(solution)/shard_map/while/body/eval_jaxpr/rev | solution.py:25
  597.9 5.8 reshape.303
  610.5 19.8 %rev.30 = f32[4,128,1152]{2,1,0:T(8,128)} reverse(f32[4,128,1152]{2,1,0:T(8,128)} %fusion.26), dimensions={2} | reverse | bytes 4718592 | tf_op jit(solution)/shard_map/while/body/eval_jaxpr/rev | solution.py:25
  646.3 19.8 %rev.30 = f32[4,128,1152]{2,1,0:T(8,128)} reverse(f32[4,128,1152]{2,1,0:T(8,128)} %fusion.26), dimensions={2} | reverse | bytes 4718592 | tf_op jit(solution)/shard_map/while/body/eval_jaxpr/rev | solution.py:25
  669.6 5.8 reshape.303
  684.2 11.9 %all-reduce.13.cloned.1.call-done = (f32[16,1024]{1,0:T(8,128)}, f32[16,1024]{1,0:T(8,128)}, f32[16,1024]{1,0:T(8,128)}, f32[16,1024]{1,0:T(8,128)}) async-done(((f32[16,1024]{1,0:T(8,128)}, f32[16,1024]{1,0:T(8,128)}, f32[16,1024]{1,0:T(8,128)}, f32[16,1024]{1,0:T(8,128)}), (f32[16,1024]{1,0:T(8,128)}, f32[16,1024]{1,0:T(8,128)}, f32[16,1024]{1,0:T(8,128)}, ...) | async-done | bytes 262160 | tf_op jit(solution)/shard_map/psum | solution.py:84
  698.3 42.0 %all-reduce.6 = (f32[16]{0:T(128)S(1)}, f32[16]{0:T(128)S(1)}) all-reduce(f32[16]{0:T(128)S(1)} %multiply_reduce_fusion.2, f32[16]{0:T(128)S(1)} %multiply_reduce_fusion.3), channel_id=1, replica_groups=mesh['tm'=16,'sec'=2] {'tm'}, use_global_device_ids=true, to_apply=%region_23.24 | all-reduce | flops 32 | bytes 256 | tf_op jit(solution)/shard_map/psum | solution.py:86
  (207 shorter events, 230.2 us)
Async XLA Ops:
  6.5 380.7 %all-reduce.15.cloned.1.call-start = ((), (), s32[]{:S(2)}) async-start(), calls=%async_computation.1 | async-start | bytes 16777216 | tf_op jit(solution)/shard_map/psum | solution.py:20
  124.2 571.9 %all-reduce.13.cloned.1.call-start = ((), (), s32[]{:S(2)}) async-start(), calls=%async_computation | async-start | bytes 524288 | tf_op jit(solution)/shard_map/psum | solution.py:84
  125.3 13.7 %collective-permute-start = (bf16[1024,128]{1,0:T(8,128)(2,1)S(1)}, bf16[1024,128]{1,0:T(8,128)(2,1)S(1)}, u32[]{:S(2)}, u32[]{:S(2)}) collective-permute-start(bf16[1024,128]{1,0:T(8,128)(2,1)S(1)} %slice.81), channel_id=1, source_target_pairs={{2,0},{4,2},{6,4},{8,6},{10,8},{12,10},{14,12},{16,14},{18,16},{20... | collective-permute-start | bytes 786440 | tf_op jit(solution)/shard_map/ppermute | solution.py:15
  423.8 1.7 slice-start
  459.6 1.7 slice-start
  495.4 1.7 slice-start
  531.3 1.7 slice-start
  567.8 1.7 slice-start.1
  603.7 1.7 slice-start.1
  639.5 1.7 slice-start.1
  675.4 1.7 slice-start.1
Sparse Core Ops, SparseCore 0:
  124.4 262.8 all-reduce.14
  678.7 17.4 all-reduce.12
where the time goes:
time: 764 us; the launch traced here: 750 us
  local copies, waits for them, and re-layouts  364 us (48%)
  waiting for transfers between devices  256 us (34%)
  blocking collectives  44.4 us (6%)
  matrix products  37.8 us (5%)
  other arithmetic  31.7 us (4%)
  between operations  14.8 us (2%)
    psum x1, waiting for transfers between devices, spread(): return lax.psum(kept, axis)  233 us
    rev x8, local copies, waits for them, and re-layouts, skew_sum(): flipped = product[:, :, ::-1]  158 us
    gather x96, local copies, waits for them, and re-layouts  99.8 us
    reshape x8, local copies, waits for them, and re-layouts, skew_sum(): widened.reshape(group_count, tap_count * (span_width + 1))  46.4 us
    psum x1, blocking collectives, finish(): power_sum = lax.psum(jnp.sum(normed * normed, axis=1), 'tm')  42 us
    dot_general x8, matrix products, one_block(): jnp.einsum('kcl,cw->klw', block, extended, preferred_element_type=jnp.flo...  34 us
    pad x8, local copies, waits for them, and re-layouts, skew_sum(): widened = jnp.pad(flipped, ((0, 0), (0, 0), (0, 1)))  27.8 us
  transfers between devices with their start and end apart: 3, of which 3 were waited for; matrix products, arithmetic and copies ran while one was open for 3% of the time, Pallas kernels for 0%

commit v1 on v0

--- a/solution.py
+++ b/solution.py
@@ -83,7 +83,7 @@
         energy_local = sliding_energy(masks, extended, lag_count, L)
         corr, energy = lax.psum((corr_local, energy_local), "sec")
         normed = corr / jnp.sqrt(energy * tmpl_power[:, None] + EPS)
-        power_sum = lax.psum(jnp.sum(normed * normed, axis=1), "tm")
+        power_sum = jnp.sum(lax.all_gather(jnp.sum(normed * normed, axis=1), "tm"), axis=0)
         meansq = power_sum / total_lags
         scored = normed / jnp.sqrt(meansq[:, None] + EPS)
         return scored

time: 764 us -> 765 us (level)
    psum x1 -> x0, blocking collectives: 42 us -> none  [finish(): power_sum = lax.psum(jnp.sum(normed * normed, axis=1), 'tm')]
    unnamed x0 -> x1, blocking collectives: none -> 42 us
where the time goes in v1:
time: 765 us; the launch traced here: 750 us
  local copies, waits for them, and re-layouts  365 us (48%)
  waiting for transfers between devices  255 us (33%)
  blocking collectives  44.4 us (6%)
  matrix products  37.8 us (5%)
  other arithmetic  31.8 us (4%)
  between operations  15.4 us (2%)
    psum x1, waiting for transfers between devices, spread(): return lax.psum(kept, axis)  233 us
    rev x8, local copies, waits for them, and re-layouts, skew_sum(): flipped = product[:, :, ::-1]  158 us
    gather x96, local copies, waits for them, and re-layouts  99.8 us
    reshape x8, local copies, waits for them, and re-layouts, skew_sum(): widened.reshape(group_count, tap_count * (span_width + 1))  46.4 us
    unnamed x1, blocking collectives  42 us
    dot_general x8, matrix products, one_block(): jnp.einsum('kcl,cw->klw', block, extended, preferred_element_type=jnp.flo...  34 us
    pad x8, local copies, waits for them, and re-layouts, skew_sum(): widened = jnp.pad(flipped, ((0, 0), (0, 0), (0, 1)))  27.8 us
  transfers between devices with their start and end apart: 3, of which 3 were waited for; matrix products, arithmetic and copies ran while one was open for 3% of the time, Pallas kernels for 0%

profile of v1, /device:TPU:0, one launch (start us, length us, event | category | flops | bytes accessed | tf_op | source)
XLA Modules:
  0.0 750.5 jit_solution(8553308981506715061)
XLA Ops:
  13.5 49.9 %while.28 = (s32[]{:T(128)}, bf16[1024,1024]{1,0:T(8,128)(2,1)}, s32[16,2]{0,1:T(2,128)S(1)}, bf16[16,1024,128]{2,1,0:T(8,128)(2,1)}, s32[]{:T(128)}) while((s32[]{:T(128)}, bf16[1024,1024]{1,0:T(8,128)(2,1)}, s32[16,2]{0,1:T(2,128)S(1)}, bf16[16,1024,128]{2,1,0:T(8,128)(2,1)}, s32[]{:T(128)}) %tuple.86), condition=%wide.while_cond, body=%wide.while_body.sunk | while | flops 2 | bytes 525401 | solution.py:58
  66.2 49.9 %while.29 = (s32[]{:T(128)}, bf16[1024,1024]{1,0:T(8,128)(2,1)}, s32[16,2]{0,1:T(2,128)S(1)}, bf16[16,1024,128]{2,1,0:T(8,128)(2,1)}, s32[]{:T(128)}) while((s32[]{:T(128)}, bf16[1024,1024]{1,0:T(8,128)(2,1)}, s32[16,2]{0,1:T(2,128)S(1)}, bf16[16,1024,128]{2,1,0:T(8,128)(2,1)}, s32[]{:T(128)}) %tuple.104), condition=%wide.while_cond.1, body=%wide.while_body.1.sunk | while | flops 2 | bytes 525401 | solution.py:58
  116.2 8.0 %select_select_fusion = (bf16[16,1024,128]{2,1,0:T(8,128)(2,1)}, bf16[16,1024,128]{2,1,0:T(8,128)(2,1)}) fusion(bf16[16,1024,128]{2,1,0:T(8,128)(2,1)} %get-tuple-element.128, pred[16,1024]{1,0:T(8,128)(4,1)S(1)} %get-tuple-element.196, pred[]{:T(512)S(6)} %eq.7, bf16[16,1024,128]{2,1,0:T(8,128)(2,1)} %get-tuple-element.120, ...), kind=kLoop, calls=%fused_computation.23 | loop fusion | flops 8388608 | bytes 16809986 | tf_op jit(solution)/shard_map/jit(_where)/select_n | solution.py:19
  129.5 9.5 %collective-permute-done = bf16[1024,128]{1,0:T(8,128)(2,1)S(1)} collective-permute-done((bf16[1024,128]{1,0:T(8,128)(2,1)S(1)}, bf16[1024,128]{1,0:T(8,128)(2,1)S(1)}, u32[]{:S(2)}, u32[]{:S(2)}) %collective-permute-start) | collective-permute-done | bytes 262176 | tf_op jit(solution)/shard_map/ppermute | solution.py:15
  154.0 233.3 %all-reduce.17.cloned.1.call-done = (bf16[16,1024,128]{2,1,0:T(8,128)(2,1)}, bf16[16,1024,128]{2,1,0:T(8,128)(2,1)}) async-done(((bf16[16,1024,128]{2,1,0:T(8,128)(2,1)}, bf16[16,1024,128]{2,1,0:T(8,128)(2,1)}), (bf16[16,1024,128]{2,1,0:T(8,128)(2,1)}, bf16[16,1024,128]{2,1,0:T(8,128)(2,1)})) %all-reduce.17.cloned.1.call-update) | async-done | bytes 8388624 | tf_op jit(solution)/shard_map/psum | solution.py:20
  390.4 143.4 %while.26 = (s32[]{:T(128)}, f32[4,4,1024]{2,1,0:T(4,128)S(1)}, bf16[4,4,1024,128]{3,2,1,0:T(8,128)(2,1)}, bf16[1024,1152]{1,0:T(8,128)(2,1)S(1)}, s32[]{:T(128)}, /*index=5*/f32[]{:T(128)}) while((s32[]{:T(128)}, f32[4,4,1024]{2,1,0:T(4,128)S(1)}, bf16[4,4,1024,128]{3,2,1,0:T(8,128)(2,1)}, bf16[1024,1152]{1,0:T(8,128)(2,1)S(1)}, s32[]{:T(128)}, ...), condition=%wide.region_3.4_spmd, body=%wide.region_1.3_spmd.sunk | while | flops 1208544768 | bytes 29483620 | solution.py:45
  394.7 19.8 %rev.28 = f32[4,128,1152]{2,1,0:T(8,128)} reverse(f32[4,128,1152]{2,1,0:T(8,128)} %fusion.23), dimensions={2} | reverse | bytes 4718592 | tf_op jit(solution)/shard_map/while/body/eval_jaxpr/rev | solution.py:25
  418.0 5.8 reshape.322
  430.6 19.8 %rev.28 = f32[4,128,1152]{2,1,0:T(8,128)} reverse(f32[4,128,1152]{2,1,0:T(8,128)} %fusion.23), dimensions={2} | reverse | bytes 4718592 | tf_op jit(solution)/shard_map/while/body/eval_jaxpr/rev | solution.py:25
  453.8 5.8 reshape.322
  466.4 19.8 %rev.28 = f32[4,128,1152]{2,1,0:T(8,128)} reverse(f32[4,128,1152]{2,1,0:T(8,128)} %fusion.23), dimensions={2} | reverse | bytes 4718592 | tf_op jit(solution)/shard_map/while/body/eval_jaxpr/rev | solution.py:25
  489.6 5.8 reshape.322
  502.3 19.8 %rev.28 = f32[4,128,1152]{2,1,0:T(8,128)} reverse(f32[4,128,1152]{2,1,0:T(8,128)} %fusion.23), dimensions={2} | reverse | bytes 4718592 | tf_op jit(solution)/shard_map/while/body/eval_jaxpr/rev | solution.py:25
  525.5 5.8 reshape.322
  534.5 143.4 %while.27 = (s32[]{:T(128)}, f32[4,4,1024]{2,1,0:T(4,128)S(1)}, bf16[4,4,1024,128]{3,2,1,0:T(8,128)(2,1)}, bf16[1024,1152]{1,0:T(8,128)(2,1)S(1)}, s32[]{:T(128)}, /*index=5*/f32[]{:T(128)}) while((s32[]{:T(128)}, f32[4,4,1024]{2,1,0:T(4,128)S(1)}, bf16[4,4,1024,128]{3,2,1,0:T(8,128)(2,1)}, bf16[1024,1152]{1,0:T(8,128)(2,1)S(1)}, ...), condition=%wide.region_15.16_spmd, body=%wide.region_13.15_spmd.sunk | while | flops 1208544768 | bytes 29483620 | solution.py:45
  538.8 19.8 %rev.30 = f32[4,128,1152]{2,1,0:T(8,128)} reverse(f32[4,128,1152]{2,1,0:T(8,128)} %fusion.26), dimensions={2} | reverse | bytes 4718592 | tf_op jit(solution)/shard_map/while/body/eval_jaxpr/rev | solution.py:25
  562.0 5.8 reshape.323
  574.6 19.8 %rev.30 = f32[4,128,1152]{2,1,0:T(8,128)} reverse(f32[4,128,1152]{2,1,0:T(8,128)} %fusion.26), dimensions={2} | reverse | bytes 4718592 | tf_op jit(solution)/shard_map/while/body/eval_jaxpr/rev | solution.py:25
  597.9 5.8 reshape.323
  610.5 19.8 %rev.30 = f32[4,128,1152]{2,1,0:T(8,128)} reverse(f32[4,128,1152]{2,1,0:T(8,128)} %fusion.26), dimensions={2} | reverse | bytes 4718592 | tf_op jit(solution)/shard_map/while/body/eval_jaxpr/rev | solution.py:25
  633.7 5.8 reshape.323
  646.3 19.8 %rev.30 = f32[4,128,1152]{2,1,0:T(8,128)} reverse(f32[4,128,1152]{2,1,0:T(8,128)} %fusion.26), dimensions={2} | reverse | bytes 4718592 | tf_op jit(solution)/shard_map/while/body/eval_jaxpr/rev | solution.py:25
  684.2 11.9 %all-reduce.15.cloned.1.call-done = (f32[16,1024]{1,0:T(8,128)}, f32[16,1024]{1,0:T(8,128)}, f32[16,1024]{1,0:T(8,128)}, f32[16,1024]{1,0:T(8,128)}) async-done(((f32[16,1024]{1,0:T(8,128)}, f32[16,1024]{1,0:T(8,128)}, f32[16,1024]{1,0:T(8,128)}, f32[16,1024]{1,0:T(8,128)}), (f32[16,1024]{1,0:T(8,128)}, f32[16,1024]{1,0:T(8,128)}, f32[16,1024]{1,0:T(8,128)}, ...) | async-done | bytes 262160 | tf_op jit(solution)/shard_map/psum | solution.py:84
  698.8 42.0 %all-reduce.8 = (f32[256]{0:T(256)S(1)}, f32[256]{0:T(256)S(1)}) all-reduce(f32[256]{0:T(256)S(1)} %dynamic-update-slice.5, f32[256]{0:T(256)S(1)} %dynamic-update-slice.4), channel_id=3, replica_groups=mesh['tm'=16,'sec'=2] {'tm'}, use_global_device_ids=true, to_apply=%add.7 | all-reduce | flops 512 | bytes 4096
  (218 shorter events, 231.5 us)
Async XLA Ops:
  6.5 380.7 %all-reduce.17.cloned.1.call-start = ((), (), s32[]{:S(2)}) async-start(), calls=%async_computation.1 | async-start | bytes 16777216 | tf_op jit(solution)/shard_map/psum | solution.py:20
  124.2 2.4 copy-start
  124.2 571.9 %all-reduce.15.cloned.1.call-start = ((), (), s32[]{:S(2)}) async-start(), calls=%async_computation | async-start | bytes 524288 | tf_op jit(solution)/shard_map/psum | solution.py:84
  125.3 13.7 %collective-permute-start = (bf16[1024,128]{1,0:T(8,128)(2,1)S(1)}, bf16[1024,128]{1,0:T(8,128)(2,1)S(1)}, u32[]{:S(2)}, u32[]{:S(2)}) collective-permute-start(bf16[1024,128]{1,0:T(8,128)(2,1)S(1)} %slice.81), channel_id=1, source_target_pairs={{2,0},{4,2},{6,4},{8,6},{10,8},{12,10},{14,12},{16,14},{18,16},{20... | collective-permute-start | bytes 786440 | tf_op jit(solution)/shard_map/ppermute | solution.py:15
  423.8 1.7 slice-start
  459.6 1.7 slice-start
  495.4 1.7 slice-start
  531.3 1.7 slice-start
  567.8 1.7 slice-start.1
  603.7 1.7 slice-start.1
  639.5 1.7 slice-start.1
  675.4 1.7 slice-start.1
Sparse Core Ops, SparseCore 0:
  124.4 262.8 all-reduce.16
  678.7 17.4 all-reduce.14
